TPU v7x, 128 devices: a whole 4x4x4 slice. The times are simulated.
128 devices in a mesh: seq: 32 (over x, y, core), fsdp: 4 (over z).
Axes of the slice: x: 4, y: 4, z: 4, core: 2. Of those that a mesh axis runs over, the one named last changes fastest.
Arguments:
- patches: bfloat16 [32768, 1280], P(('seq', 'fsdp')), may hold values from -6 to 6
- vis_index: int32 [32768], P(('seq', 'fsdp')), may hold values from 0 to 131071, as said below
- kv_list: int32 [256, 16], P(('seq', 'fsdp')), may hold values from 0 to 255, as said below
- kv_count: int32 [256], P(('seq', 'fsdp')), may hold values from 1 to 16, as said below
- global_tiles: int32 [2], replicated, may hold values from 0 to 255
- frame_table: bfloat16 [256, 1280], replicated, may hold values from -3 to 3
- space_table: bfloat16 [512, 1280], replicated, may hold values from -3 to 3
- ln_gain: bfloat16 [1280], replicated, may hold values from 0.25 to 1.75
- ln_bias: bfloat16 [1280], replicated, may hold values from -3 to 3
- w_qkv: bfloat16 [1280, 3840], P('fsdp')
- w_out: bfloat16 [1280, 1280], P('fsdp'), may hold values from -1.25 to 1.25
Outputs:
- attended: bfloat16 [32768, 1280], P(('seq', 'fsdp'))
Inputs may be any that keep to these rules, and one draw needn't show every extreme that they name: `vis_index`: exactly one visible position in each aligned group of four; strictly increasing. `kv_list`: the first entry of query tile i is i itself; entries may repeat; every entry t satisfies |t // 8 - i // 8| <= 2. Over all entries of an aligned run of 2 query tiles, the tiles that lie in any one group other than the run's own group (group = tile // 8) number at most 3 distinct ones, and exactly 3 for every such group within two of the run's own. On every device at least one query tile has kv_count = 16.
All inputs are finite; a program needn't handle non-finite values.
Results may differ from a plain program's by a relative error of at most 0.0065.
Values may be sent and summed in bfloat16 or wider, within the bound.
No kernel may reach another device: no remote copies, remote signals or barrier semaphores. Data moves between devices by JAX's collectives and lax.ppermute only.
A program may use at most 192 MiB of HBM per device.

v0:
```python
import jax
import jax.numpy as jnp
from jax import lax
from jax.sharding import PartitionSpec as P

HEADS = 16
TILE = 128
KT = 16
GLOBAL = 2
PATCHES = 512
NEAR = 3
REACH = (-2, -1, 1, 2)


def passed_along(block, axis, distance):
    devices = range(lax.axis_size(axis))
    route = [(i - distance, i) for i in devices if i - distance in devices]
    return lax.ppermute(block, axis, route)


def layer_norm(stream, ln_gain, ln_bias):
    stream32 = stream.astype(jnp.float32)
    mean_val = jnp.mean(stream32, axis=-1, keepdims=True)
    centred = stream32 - mean_val
    variance = jnp.mean(centred * centred, axis=-1, keepdims=True)
    scaled = centred * lax.rsqrt(variance + 1e-06)
    return (scaled * ln_gain.astype(jnp.float32) + ln_bias.astype(jnp.float32)).astype(jnp.bfloat16)


def embed(patches, vis_index, frame_table, space_table):
    frame_ids = vis_index // PATCHES
    patch_ids = vis_index % PATCHES
    return (
        patches.astype(jnp.float32)
        + frame_table[frame_ids].astype(jnp.float32)
        + space_table[patch_ids].astype(jnp.float32)
    ).astype(jnp.bfloat16)


def near_tiles(entries, group, group_tiles):
    cand = group * group_tiles + jnp.arange(group_tiles, dtype=jnp.int32)
    named = jnp.any(entries.reshape(-1, 1) == cand[None, :], axis=0)
    rank = jnp.cumsum(named.astype(jnp.int32)) - 1
    local_ids = jnp.arange(group_tiles, dtype=jnp.int32)
    picks = jnp.stack([jnp.sum(jnp.where(named & (rank == j), local_ids, 0)) for j in range(NEAR)])
    return (picks, rank)


def attend_tile(query_tile, key_values, key_live, feat_width):
    head_size = feat_width // HEADS
    key_rows = key_values.shape[0]
    queries_h = query_tile.reshape(TILE, HEADS, head_size)
    keys_h = key_values[:, :feat_width].reshape(key_rows, HEADS, head_size)
    values_h = key_values[:, feat_width:].reshape(key_rows, HEADS, head_size)
    scores = jnp.einsum(
        "qhd,khd->hqk", queries_h, keys_h, preferred_element_type=jnp.float32
    ) * head_size ** (-0.5)
    scores = jnp.where(key_live[None, None, :], scores, -jnp.inf)
    row_max = jnp.max(scores, axis=-1, keepdims=True)
    weights_raw = jnp.exp(scores - row_max)
    probs = (weights_raw / jnp.sum(weights_raw, axis=-1, keepdims=True)).astype(jnp.bfloat16)
    mixed_h = jnp.einsum("hqk,khd->qhd", probs, values_h, preferred_element_type=jnp.float32)
    return mixed_h.reshape(TILE, feat_width).astype(jnp.bfloat16)


def local(
    patches,
    vis_index,
    kv_list,
    kv_count,
    global_tiles,
    frame_table,
    space_table,
    ln_gain,
    ln_bias,
    w_qkv,
    w_out,
):
    tok_rows = patches.shape[0]
    feat_width = patches.shape[1]
    tile_count = tok_rows // TILE
    fsdp_size = lax.axis_size("fsdp")
    seq_size = lax.axis_size("seq")
    seq_at = lax.axis_index("seq")
    dev_at = seq_at * fsdp_size + lax.axis_index("fsdp")
    group_tiles = tile_count * fsdp_size
    stream = embed(patches, vis_index, frame_table, space_table)
    global_rows = []
    for slot_no in range(GLOBAL):
        tile_id = global_tiles[slot_no]
        mine = tile_id // tile_count == dev_at
        rows = lax.dynamic_slice_in_dim(stream, tile_id % tile_count * TILE, TILE, 0)
        global_rows.append(jnp.where(mine, rows, jnp.zeros_like(rows)))
    global_stream = lax.psum(jnp.concatenate(global_rows, axis=0), ("seq", "fsdp"))
    w_full = lax.all_gather(w_qkv, "fsdp", axis=0, tiled=True)
    normed = layer_norm(stream, ln_gain, ln_bias)
    qkv = jnp.dot(normed, w_full, preferred_element_type=jnp.float32).astype(jnp.bfloat16)
    query = qkv[:, :feat_width]
    keyval = qkv[:, feat_width:]
    global_normed = layer_norm(global_stream, ln_gain, ln_bias)
    global_kv = (
        jnp.dot(global_normed, w_full[:, feat_width:], preferred_element_type=jnp.float32)
        .astype(jnp.bfloat16)
        .reshape(GLOBAL, TILE, 2 * feat_width)
    )
    group_block = lax.all_gather(keyval, "fsdp", axis=0, tiled=True).reshape(
        group_tiles, TILE, 2 * feat_width
    )
    seq_lists = lax.all_gather(kv_list, "seq", axis=0, tiled=True)
    near_blocks = []
    near_rank = []
    for reach in REACH:
        distance = -reach
        dest = jnp.clip(seq_at + distance, 0, seq_size - 1)
        dest_lists = lax.dynamic_slice_in_dim(seq_lists, dest * tile_count, tile_count, 0)
        send_ids, unused = near_tiles(dest_lists, seq_at, group_tiles)
        sent = passed_along(group_block[send_ids], "seq", distance)
        near_blocks.append(sent)
        unused2, rank = near_tiles(kv_list, seq_at + reach, group_tiles)
        near_rank.append(rank)
    window = jnp.concatenate([group_block] + near_blocks + [global_kv], axis=0)
    near_rank = jnp.stack(near_rank)
    entry_group = kv_list // group_tiles
    entry_local = kv_list % group_tiles
    reach_of = entry_group - seq_at
    reach_slot = jnp.where(reach_of < 0, reach_of + 2, reach_of + 1)
    reach_slot = jnp.clip(reach_slot, 0, len(REACH) - 1)
    entry_rank = near_rank[reach_slot, entry_local]
    local_lists = jnp.where(
        reach_of == 0, entry_local, group_tiles + NEAR * reach_slot + entry_rank
    )
    global_slots = group_tiles + NEAR * len(REACH) + jnp.arange(GLOBAL, dtype=jnp.int32)
    query_tiles = query.reshape(tile_count, TILE, feat_width)

    def per_tile(tile_args):
        query_tile, local_ids, live_count = tile_args
        slot_live_row = jnp.concatenate(
            [jnp.arange(KT) < live_count, jnp.ones((GLOBAL,), dtype=bool)]
        )
        key_live = jnp.repeat(slot_live_row, TILE)
        key_values = window[jnp.concatenate([local_ids, global_slots])].reshape(
            (KT + GLOBAL) * TILE, 2 * feat_width
        )
        return attend_tile(query_tile, key_values, key_live, feat_width)

    heads_out = lax.map(per_tile, (query_tiles, local_lists, kv_count)).reshape(
        tok_rows, feat_width
    )
    return jnp.dot(
        heads_out,
        lax.all_gather(w_out, "fsdp", axis=0, tiled=True),
        preferred_element_type=jnp.float32,
    ).astype(jnp.bfloat16)


def solution(mesh):
    return jax.shard_map(
        local,
        mesh=mesh,
        in_specs=(
            P(("seq", "fsdp"), None),
            P(("seq", "fsdp")),
            P(("seq", "fsdp"), None),
            P(("seq", "fsdp")),
            P(),
            P(),
            P(),
            P(),
            P(),
            P("fsdp", None),
            P("fsdp", None),
        ),
        out_specs=P(("seq", "fsdp"), None),
        check_vma=False,
    )
```

profile of v0, /device:TPU:28, one launch (start us, length us, event | category | flops | bytes accessed | tf_op | source)
XLA Modules:
  0.0 548.4 jit_solution(2590682510310247328)
XLA Ops:
  10.2 1.3 gather_fusion.2
  11.5 1.2 gather_fusion.3
  13.5 93.8 %all-gather.5.cloned.1.call-done = bf16[1280,3840]{1,0:T(8,128)(2,1)} async-done(((bf16[320,3840]{1,0:T(8,128)(2,1)}), bf16[1280,3840]{1,0:T(8,128)(2,1)}) %all-gather.5.cloned.1.call-update) | async-done | bytes 9830416 | tf_op jit(solution)/shard_map/all_gather | solution.py:95
  107.2 6.6 %convolution_convert_fusion = bf16[256,3840]{1,0:T(8,128)(2,1)S(1)} fusion(bf16[1280,3840]{1,0:T(8,128)(2,1)} %all-gather.5.cloned.1.call-done, bf16[256,1280]{1,0:T(8,128)(2,1)S(1)} %get-tuple-element.114, f32[1280]{0:T(1024)S(1)} %convert_element_type.182, f32[1280]{0:T(1024)S(1)} %convert_element_type.181, f32[256]{0:T(256)S(1)} %add_rsqrt_fusion.1, ...), kind=kOutput, calls=%fused_computation.34 | convolution fusion | flops 2519531520 | bytes 12464128 | tf_op jit(solution)/shard_map/dot_general | solution.py:97
  113.9 1.2 copy-done.4
  115.2 1.2 slice.46
  122.4 0.9 pad_maximum_fusion
  124.1 22.4 %all-gather = s32[32,2,16]{2,1,0:T(2,128)S(1)} all-gather(s32[1,2,16]{2,1,0:T(2,128)S(1)} %bitcast.181), channel_id=1, replica_groups=mesh['seq'=32,'fsdp'=4] {'seq'}, dimensions={0}, use_global_device_ids=true | all-gather | bytes 4224 | tf_op jit(solution)/shard_map/all_gather | solution.py:109
  147.3 0.7 fusion.65
  148.2 0.7 fusion.68
  148.9 3.8 fusion.61
  152.9 0.7 fusion.71
  153.9 0.7 fusion.74
  154.6 3.8 fusion.63
  159.5 0.8 gather_fusion.1
  160.4 14.5 %all-gather.7.cloned.1.call-done = bf16[1024,2560]{1,0:T(8,128)(2,1)} async-done(((bf16[256,2560]{1,0:T(8,128)(2,1)}), bf16[1024,2560]{1,0:T(8,128)(2,1)}) %all-gather.7.cloned.1.call-update) | async-done | bytes 5242896 | tf_op jit(solution)/shard_map/all_gather | solution.py:106
  174.9 4.6 gather_fusion.4
  179.5 3.0 collective-permute-start
  182.5 137.3 %all-reduce.3.cloned.1.call-done = bf16[256,1280]{1,0:T(8,128)(2,1)} async-done(((bf16[256,1280]{1,0:T(8,128)(2,1)}), bf16[256,1280]{1,0:T(8,128)(2,1)}) %all-reduce.3.cloned.1.call-update) | async-done | bytes 655376 | tf_op jit(solution)/shard_map/psum | solution.py:94
  319.8 1.3 convert_reduce_fusion
  321.2 4.5 gather_fusion.5
  325.7 2.1 collective-permute-start.1
  328.1 4.6 gather_fusion.6
  332.7 3.4 collective-permute-start.2
  336.2 4.7 gather_fusion.7
  340.9 2.6 collective-permute-start.3
  343.5 4.8 fusion.17
  348.7 1.7 constant_dynamic-update-slice_fusion.5
  350.4 1.6 collective-permute-done.1
  351.9 1.7 constant_dynamic-update-slice_fusion.4
  353.6 19.3 %collective-permute-done.2 = bf16[3,128,2560]{2,1,0:T(8,128)(2,1)} collective-permute-done((bf16[3,128,2560]{2,1,0:T(8,128)(2,1)}, bf16[3,128,2560]{2,1,0:T(8,128)(2,1)}, u32[]{:S(2)}, u32[]{:S(2)}) %collective-permute-start.2) | collective-permute-done | bytes 1966112 | tf_op jit(solution)/shard_map/ppermute | solution.py:18
  373.0 1.7 constant_dynamic-update-slice_fusion.3
  374.7 30.7 %collective-permute-done.3 = bf16[3,128,2560]{2,1,0:T(8,128)(2,1)S(1)} collective-permute-done((bf16[3,128,2560]{2,1,0:T(8,128)(2,1)}, bf16[3,128,2560]{2,1,0:T(8,128)(2,1)S(1)}, u32[]{:S(2)}, u32[]{:S(2)}) %collective-permute-start.3) | collective-permute-done | bytes 1966112 | tf_op jit(solution)/shard_map/ppermute | solution.py:18
  405.6 5.0 copy-done.2
  410.6 126.7 %while.11 = (s32[]{:T(128)}, bf16[2,128,1280]{2,1,0:T(8,128)(2,1)S(1)}, s32[2,16]{1,0:T(2,128)S(1)}, bf16[22,128,2560]{2,1,0:T(8,128)(2,1)}, s32[2]{0:T(128)S(1)...) while((s32[]{:T(128)}, bf16[2,128,1280]{2,1,0:T(8,128)(2,1)S(1)}, ...), condition=%wide.region_36.37_spmd.clone, body=%wide.region_33.36_spmd.clone.sunk | while | flops 1538428160 | bytes 123626584 | solution.py:146
  410.7 11.3 %gather_fusion = bf16[18,128,2560]{2,1,0:T(8,128)(2,1)} fusion(bf16[22,128,2560]{2,1,0:T(8,128)(2,1)} %get-tuple-element.205, s32[1024]{0:T(1024)S(1)} %pad_clamp_fusion.8), kind=kCustom, calls=%fused_computation.clone.clone.1 | custom fusion | bytes 23593032 | tf_op jit(solution)/shard_map/while/body/eval_jaxpr/gather | solution.py:141
  422.0 9.7 %fusion.102 = (bf16[2304,1280]{1,0:T(8,128)(2,1)}, bf16[2304,1280]{1,0:T(8,128)(2,1)}) fusion(bf16[2304,2560]{1,0:T(8,128)(2,1)} %bitcast.166), kind=kLoop, calls=%fused_computation.186.clone.1 | loop fusion | bytes 23592960 | tf_op jit(solution)/shard_map/while/body/eval_jaxpr/slice | solution.py:53
  431.7 8.9 %copy.38 = bf16[2304,1280]{0,1:T(8,128)(2,1)} copy(bf16[2304,1280]{1,0:T(8,128)(2,1)} %get-tuple-element.183) | data formatting | bytes 11796480 | tf_op jit(solution)/shard_map/while
  442.1 11.3 %fusion.103 = (f32[16,128]{1,0:T(8,128)S(1)}, f32[16,128,2304]{2,1,0:T(8,128)}) fusion(pred[2304]{0:T(1024)(128)(4,1)S(1)} %broadcast_bitcast_fusion.2, bf16[128,16,80]{0,2,1:T(8,128)(2,1)S(1)} %bitcast.176, bf16[2304,16,80]{0,2,1:T(8,128)(2,1)} %bitcast.167), kind=kOutput, calls=%fused_computation.187.clone.1 | convolution fusion | flops 773851392 | bytes 25110784 | tf_op jit(solution)/shard_map/while/body/eval_jaxpr/sub | solution.py:60
  453.4 8.9 %copy.36 = bf16[2304,1280]{0,1:T(8,128)(2,1)} copy(bf16[2304,1280]{1,0:T(8,128)(2,1)} %get-tuple-element.182) | data formatting | bytes 11796480 | tf_op jit(solution)/shard_map/while
  462.2 11.5 %fusion.104 = bf16[16,80,128]{2,1,0:T(8,128)(2,1)S(1)} fusion(bf16[2304,16,80]{0,2,1:T(8,128)(2,1)} %bitcast.168, f32[16,128,2304]{2,1,0:T(8,128)} %get-tuple-element.184, f32[16,128]{1,0:T(8,128)S(1)} %get-tuple-element.185), kind=kOutput, calls=%fused_computation.19.clone.1 | convolution fusion | flops 764575744 | bytes 25108480 | tf_op jit(solution)/shard_map/while/body/eval_jaxpr/hqk,khd->qhd/dot_general | solution.py:62
  474.1 11.3 %gather_fusion = bf16[18,128,2560]{2,1,0:T(8,128)(2,1)} fusion(bf16[22,128,2560]{2,1,0:T(8,128)(2,1)} %get-tuple-element.205, s32[1024]{0:T(1024)S(1)} %pad_clamp_fusion.8), kind=kCustom, calls=%fused_computation.clone.clone.1 | custom fusion | bytes 23593032 | tf_op jit(solution)/shard_map/while/body/eval_jaxpr/gather | solution.py:141
  485.4 9.7 %fusion.102 = (bf16[2304,1280]{1,0:T(8,128)(2,1)}, bf16[2304,1280]{1,0:T(8,128)(2,1)}) fusion(bf16[2304,2560]{1,0:T(8,128)(2,1)} %bitcast.166), kind=kLoop, calls=%fused_computation.186.clone.1 | loop fusion | bytes 23592960 | tf_op jit(solution)/shard_map/while/body/eval_jaxpr/slice | solution.py:53
  495.0 8.9 %copy.38 = bf16[2304,1280]{0,1:T(8,128)(2,1)} copy(bf16[2304,1280]{1,0:T(8,128)(2,1)} %get-tuple-element.183) | data formatting | bytes 11796480 | tf_op jit(solution)/shard_map/while
  505.5 11.3 %fusion.103 = (f32[16,128]{1,0:T(8,128)S(1)}, f32[16,128,2304]{2,1,0:T(8,128)}) fusion(pred[2304]{0:T(1024)(128)(4,1)S(1)} %broadcast_bitcast_fusion.2, bf16[128,16,80]{0,2,1:T(8,128)(2,1)S(1)} %bitcast.176, bf16[2304,16,80]{0,2,1:T(8,128)(2,1)} %bitcast.167), kind=kOutput, calls=%fused_computation.187.clone.1 | convolution fusion | flops 773851392 | bytes 25110784 | tf_op jit(solution)/shard_map/while/body/eval_jaxpr/sub | solution.py:60
  516.7 8.9 %copy.36 = bf16[2304,1280]{0,1:T(8,128)(2,1)} copy(bf16[2304,1280]{1,0:T(8,128)(2,1)} %get-tuple-element.182) | data formatting | bytes 11796480 | tf_op jit(solution)/shard_map/while
  525.6 11.5 %fusion.104 = bf16[16,80,128]{2,1,0:T(8,128)(2,1)S(1)} fusion(bf16[2304,16,80]{0,2,1:T(8,128)(2,1)} %bitcast.168, f32[16,128,2304]{2,1,0:T(8,128)} %get-tuple-element.184, f32[16,128]{1,0:T(8,128)S(1)} %get-tuple-element.185), kind=kOutput, calls=%fused_computation.19.clone.1 | convolution fusion | flops 764575744 | bytes 25108480 | tf_op jit(solution)/shard_map/while/body/eval_jaxpr/hqk,khd->qhd/dot_general | solution.py:62
  537.4 3.9 convolution_convert_fusion.1
  (116 shorter events, 12.4 us)
Async XLA Ops:
  7.4 4.1 copy-start
  7.4 2.8 copy-start.3
  7.4 99.9 %all-gather.5.cloned.1.call-start = ((), (), s32[]{:S(2)}) async-start(), calls=%async_computation | async-start | bytes 12288000 | tf_op jit(solution)/shard_map/all_gather | solution.py:95
  8.1 166.8 %all-gather.7.cloned.1.call-start = ((), (), s32[]{:S(2)}) async-start(), calls=%async_computation.1 | async-start | bytes 6553600 | tf_op jit(solution)/shard_map/all_gather | solution.py:106
  11.5 1.3 copy-start.6
  113.9 1.3 copy-start.4
  115.1 1.2 copy-start.8
  116.3 7.7 %copy-start.7 = (s32[2,16]{1,0:T(2,128)S(1)}, s32[2,16]{1,0:T(2,128)}, u32[]{:S(2)}) copy-start(s32[2,16]{1,0:T(2,128)} %param.15) | copy-start | bytes 388
  116.3 203.5 %all-reduce.3.cloned.1.call-start = ((), (), s32[]{:S(2)}) async-start(), calls=%async_computation.2 | async-start | bytes 1310720 | tf_op jit(solution)/shard_map/psum | solution.py:94
  123.3 414.2 %all-gather.9.cloned.1.call-start = ((), (), s32[]{:S(2)}) async-start(), calls=%async_computation.3 | async-start | bytes 4096000 | tf_op jit(solution)/shard_map/all_gather | solution.py:151
  179.5 169.2 %collective-permute-start = (bf16[3,128,2560]{2,1,0:T(8,128)(2,1)}, bf16[3,128,2560]{2,1,0:T(8,128)(2,1)}, u32[]{:S(2)}, u32[]{:S(2)}) collective-permute-start(bf16[3,128,2560]{2,1,0:T(8,128)(2,1)} %gather_fusion.4), channel_id=1, source_target_pairs={{0,8},{4,12},{8,16},{12,20},{16,24},{20,28},{24,32},{28,36},{32,40... | collective-permute-start | bytes 5898248 | tf_op jit(solution)/shard_map/ppermute | solution.py:18
  319.8 8.0 %copy-start.5 = (bf16[256,1280]{1,0:T(8,128)(2,1)S(1)}, bf16[256,1280]{1,0:T(8,128)(2,1)}, u32[]{:S(2)}) copy-start(bf16[256,1280]{1,0:T(8,128)(2,1)} %all-reduce.3.cloned.1.call-done) | copy-start | bytes 1966084
  325.7 26.3 %collective-permute-start.1 = (bf16[3,128,2560]{2,1,0:T(8,128)(2,1)}, bf16[3,128,2560]{2,1,0:T(8,128)(2,1)}, u32[]{:S(2)}, u32[]{:S(2)}) collective-permute-start(bf16[3,128,2560]{2,1,0:T(8,128)(2,1)} %gather_fusion.5), channel_id=1, source_target_pairs={{0,4},{4,8},{8,12},{12,16},{16,20},{20,24},{24,28},{28,32},{32,36}... | collective-permute-start | bytes 5898248 | tf_op jit(solution)/shard_map/ppermute | solution.py:18
  332.7 40.3 %collective-permute-start.2 = (bf16[3,128,2560]{2,1,0:T(8,128)(2,1)}, bf16[3,128,2560]{2,1,0:T(8,128)(2,1)}, u32[]{:S(2)}, u32[]{:S(2)}) collective-permute-start(bf16[3,128,2560]{2,1,0:T(8,128)(2,1)} %gather_fusion.6), channel_id=1, source_target_pairs={{4,0},{8,4},{12,8},{16,12},{20,16},{24,20},{28,24},{32,28},{36,32}... | collective-permute-start | bytes 5898248 | tf_op jit(solution)/shard_map/ppermute | solution.py:18
  336.2 12.2 %slice-start = ((s8[5242880]{0:T(1024)(128)(4,1)}), s8[1048576]{0:T(1024)(128)(4,1)S(1)}, s32[]{:S(2)}) async-start(s8[5242880]{0:T(1024)(128)(4,1)} %bitcast.173), calls=%async_computation.4 | async-start | bytes 2097152
  340.9 7.5 %slice-start.1 = ((s8[5242880]{0:T(1024)(128)(4,1)}), s8[4194304]{0:T(1024)(128)(4,1)S(1)}, s32[]{:S(2)}) async-start(s8[5242880]{0:T(1024)(128)(4,1)} %bitcast.173), calls=%async_computation.5 | async-start | bytes 8388608
  340.9 64.5 %collective-permute-start.3 = (bf16[3,128,2560]{2,1,0:T(8,128)(2,1)}, bf16[3,128,2560]{2,1,0:T(8,128)(2,1)S(1)}, u32[]{:S(2)}, u32[]{:S(2)}) collective-permute-start(bf16[3,128,2560]{2,1,0:T(8,128)(2,1)} %gather_fusion.7), channel_id=1, source_target_pairs={{8,0},{12,4},{16,8},{20,12},{24,16},{28,20},{32,24},{36,28},{40,32... | collective-permute-start | bytes 5898248 | tf_op jit(solution)/shard_map/ppermute | solution.py:18
  374.6 36.0 %slice-start.2 = ((bf16[256,3840]{1,0:T(8,128)(2,1)}), bf16[256,1280]{1,0:T(8,128)(2,1)S(1)}, s32[]{:S(2)}) async-start(bf16[256,3840]{1,0:T(8,128)(2,1)} %copy-done.4), calls=%async_computation.6 | async-start | bytes 1310720 | tf_op jit(solution)/shard_map/slice | solution.py:98
  374.6 36.0 %copy-start.9 = (s32[2]{0:T(128)S(1)}, s32[2]{0:T(128)}, u32[]{:S(2)}) copy-start(s32[2]{0:T(128)} %param.16) | copy-start | bytes 28
  405.6 5.0 copy-start.2
  537.4 3.9 copy-start.1
Sparse Core Ops, SparseCore 0:
  9.8 97.3 all-gather.4
  116.5 58.4 all-gather.6
  176.6 41.3 all-gather.8
Sparse Core Ops, SparseCore 1:
  123.3 196.4 all-reduce.2
where the time goes:
time: 550 us; the launch traced here: 548 us
  waiting for transfers between devices  299 us (54%)
  local copies, waits for them, and re-layouts  115 us (21%)
  matrix products  61 us (11%)
  blocking collectives  22.4 us (4%)
  between operations  20.2 us (4%)
  other arithmetic  19.5 us (4%)
  starting transfers between devices  11.3 us (2%)
    psum x1, waiting for transfers between devices, local(): lax.psum(jnp.concatenate(global_rows, axis=0), ('seq', 'fsdp'))  137 us
    all_gather x1, waiting for transfers between devices, local(): w_full = lax.all_gather(w_qkv, 'fsdp', axis=0, tiled=True)  93.8 us
    ppermute x4, waiting for transfers between devices, passed_along(): return lax.ppermute(block, axis, route)  51.6 us
    while x4, local copies, waits for them, and re-layouts  35.4 us
    dot_general x2, matrix products, attend_tile(): jnp.einsum('hqk,khd->qhd', probs, values_h, preferred_element_type=jnp.fl...  23.1 us
    sub x2, matrix products, attend_tile(): weights_raw = jnp.exp(scores - row_max)  22.6 us
    gather x2, local copies, waits for them, and re-layouts, per_tile(): window[jnp.concatenate([local_ids, global_slots])]  22.5 us
    all_gather x1, blocking collectives, local(): seq_lists = lax.all_gather(kv_list, 'seq', axis=0, tiled=True)  22.4 us
  transfers between devices with their start and end apart: 8, of which 6 were waited for; matrix products, arithmetic and copies ran while one was open for 32% of the time, Pallas kernels for 0%

commit v1 on v0

--- a/solution.py
+++ b/solution.py
@@ -91,7 +91,9 @@
         mine = tile_id // tile_count == dev_at
         rows = lax.dynamic_slice_in_dim(stream, tile_id % tile_count * TILE, TILE, 0)
         global_rows.append(jnp.where(mine, rows, jnp.zeros_like(rows)))
-    global_stream = lax.psum(jnp.concatenate(global_rows, axis=0), ("seq", "fsdp"))
+    block_2 = jnp.concatenate(global_rows, axis=0)
+    parts = lax.all_gather(block_2, ("seq", "fsdp"), axis=0, tiled=False)
+    global_stream = parts.sum(axis=0)
     w_full = lax.all_gather(w_qkv, "fsdp", axis=0, tiled=True)
     normed = layer_norm(stream, ln_gain, ln_bias)
     qkv = jnp.dot(normed, w_full, preferred_element_type=jnp.float32).astype(jnp.bfloat16)

time: 550 us -> 610 us (1.11)
  other arithmetic: 19.5 us -> 45.8 us
  waiting for transfers between devices: 299 us -> 325 us
  local copies, waits for them, and re-layouts: 115 us -> 122 us
    all_gather x0 -> x1, waiting for transfers between devices: none -> 167 us  [local(): parts = lax.all_gather(block_2, ('seq', 'fsdp'), axis=0, tiled=False)]
    psum x1 -> x0, waiting for transfers between devices: 137 us -> none  [local(): lax.psum(jnp.concatenate(global_rows, axis=0), ('seq', 'fsdp'))]
    reduce_sum x0 -> x1, other arithmetic: none -> 27.5 us  [local(): global_stream = parts.sum(axis=0)]
    unnamed x29 -> x23, local copies, waits for them, and re-layouts: 11.8 us -> 17.1 us
  transfers between devices with their start and end apart: 8 -> 8, of which waited for: 6 -> 6; matrix products, arithmetic and copies ran while one was open for 32% -> 36% of each run, Pallas kernels for 0% -> 0%
where the time goes in v1:
time: 610 us; the launch traced here: 607 us
  waiting for transfers between devices  325 us (53%)
  local copies, waits for them, and re-layouts  122 us (20%)
  matrix products  61.2 us (10%)
  other arithmetic  45.8 us (8%)
  blocking collectives  22.3 us (4%)
  between operations  18.7 us (3%)
  starting transfers between devices  11.5 us (2%)
    all_gather x1, waiting for transfers between devices, local(): parts = lax.all_gather(block_2, ('seq', 'fsdp'), axis=0, tiled=False)  167 us
    all_gather x1, waiting for transfers between devices, local(): w_full = lax.all_gather(w_qkv, 'fsdp', axis=0, tiled=True)  93.7 us
    ppermute x4, waiting for transfers between devices, passed_along(): return lax.ppermute(block, axis, route)  46.9 us
    while x4, local copies, waits for them, and re-layouts  35.5 us
    reduce_sum x1, other arithmetic, local(): global_stream = parts.sum(axis=0)  27.5 us
    dot_general x2, matrix products, attend_tile(): jnp.einsum('hqk,khd->qhd', probs, values_h, preferred_element_type=jnp.fl...  23.1 us
    sub x2, matrix products, attend_tile(): weights_raw = jnp.exp(scores - row_max)  22.6 us
    gather x2, local copies, waits for them, and re-layouts, per_tile(): window[jnp.concatenate([local_ids, global_slots])]  22.5 us
  transfers between devices with their start and end apart: 8, of which 6 were waited for; matrix products, arithmetic and copies ran while one was open for 36% of the time, Pallas kernels for 0%

profile of v1, /device:TPU:28, one launch (start us, length us, event | category | flops | bytes accessed | tf_op | source)
XLA Modules:
  0.0 606.9 jit_solution(290512045069562858)
XLA Ops:
  7.3 0.7 convert_element_type.183
  9.5 1.2 gather_fusion.3
  10.7 1.3 gather_fusion.2
  12.7 93.7 %all-gather.7.cloned.1.call-done = bf16[1280,3840]{1,0:T(8,128)(2,1)} async-done(((bf16[320,3840]{1,0:T(8,128)(2,1)}), bf16[1280,3840]{1,0:T(8,128)(2,1)}) %all-gather.7.cloned.1.call-update) | async-done | bytes 9830416 | tf_op jit(solution)/shard_map/all_gather | solution.py:97
  106.4 6.6 %convolution_convert_fusion = bf16[256,3840]{1,0:T(8,128)(2,1)S(1)} fusion(bf16[1280,3840]{1,0:T(8,128)(2,1)} %all-gather.7.cloned.1.call-done, bf16[256,1280]{1,0:T(8,128)(2,1)S(1)} %get-tuple-element.114, f32[1280]{0:T(1024)S(1)} %convert_element_type.184, f32[1280]{0:T(1024)S(1)} %convert_element_type.183, f32[256]{0:T(256)S(1)} %add_rsqrt_fusion.1, ...), kind=kOutput, calls=%fused_computation.34 | convolution fusion | flops 2519531520 | bytes 12464128 | tf_op jit(solution)/shard_map/dot_general | solution.py:99
  113.1 1.3 slice.46
  120.3 0.9 pad_maximum_fusion
  122.4 22.3 %all-gather.1 = s32[32,2,16]{2,1,0:T(2,128)S(1)} all-gather(s32[1,2,16]{2,1,0:T(2,128)S(1)} %bitcast.180), channel_id=1, replica_groups=mesh['seq'=32,'fsdp'=4] {'seq'}, dimensions={0}, use_global_device_ids=true | all-gather | bytes 4224 | tf_op jit(solution)/shard_map/all_gather | solution.py:111
  146.8 0.7 fusion.71
  148.2 0.7 fusion.74
  148.9 3.8 fusion.61
  152.7 3.9 fusion.63
  156.6 16.0 %all-gather.9.cloned.1.call-done = bf16[1024,2560]{1,0:T(8,128)(2,1)} async-done(((bf16[256,2560]{1,0:T(8,128)(2,1)}), bf16[1024,2560]{1,0:T(8,128)(2,1)}) %all-gather.9.cloned.1.call-update) | async-done | bytes 5242896 | tf_op jit(solution)/shard_map/all_gather | solution.py:108
  172.6 4.5 gather_fusion.4
  177.1 3.0 collective-permute-start
  180.5 4.5 gather_fusion.5
  185.0 1.9 collective-permute-start.1
  187.0 4.8 gather_fusion.6
  191.7 3.4 collective-permute-start.2
  195.4 4.6 gather_fusion.7
  200.1 3.0 collective-permute-start.3
  203.1 0.8 gather_fusion.1
  204.0 5.2 constant_dynamic-update-slice_fusion.6
  209.1 22.9 %collective-permute-done = bf16[3,128,2560]{2,1,0:T(8,128)(2,1)} collective-permute-done((bf16[3,128,2560]{2,1,0:T(8,128)(2,1)}, bf16[3,128,2560]{2,1,0:T(8,128)(2,1)}, u32[]{:S(2)}, u32[]{:S(2)}) %collective-permute-start) | collective-permute-done | bytes 1966112 | tf_op jit(solution)/shard_map/ppermute | solution.py:18
  232.0 3.0 constant_dynamic-update-slice_fusion.5
  235.0 16.8 %collective-permute-done.1 = bf16[3,128,2560]{2,1,0:T(8,128)(2,1)} collective-permute-done((bf16[3,128,2560]{2,1,0:T(8,128)(2,1)}, bf16[3,128,2560]{2,1,0:T(8,128)(2,1)}, u32[]{:S(2)}, u32[]{:S(2)}) %collective-permute-start.1) | collective-permute-done | bytes 1966112 | tf_op jit(solution)/shard_map/ppermute | solution.py:18
  251.8 3.0 constant_dynamic-update-slice_fusion.4
  254.8 2.9 constant_dynamic-update-slice_fusion.3
  257.7 7.2 %collective-permute-done.3 = bf16[3,128,2560]{2,1,0:T(8,128)(2,1)} collective-permute-done((bf16[3,128,2560]{2,1,0:T(8,128)(2,1)}, bf16[3,128,2560]{2,1,0:T(8,128)(2,1)}, u32[]{:S(2)}, u32[]{:S(2)}) %collective-permute-start.3) | collective-permute-done | bytes 1966112 | tf_op jit(solution)/shard_map/ppermute | solution.py:18
  264.9 3.0 constant_dynamic-update-slice_fusion.2
  267.9 167.1 %all-gather.13.cloned.1.call-done = bf16[32768,1280]{1,0:T(8,128)(2,1)} async-done(((bf16[256,1280]{1,0:T(8,128)(2,1)}), bf16[32768,1280]{1,0:T(8,128)(2,1)}) %all-gather.13.cloned.1.call-update) | async-done | bytes 83886096 | tf_op jit(solution)/shard_map/all_gather | solution.py:95
  435.0 27.5 %reduce_sum.179 = bf16[256,1280]{1,0:T(8,128)(2,1)S(1)} reduce(bf16[128,256,1280]{2,1,0:T(8,128)(2,1)} %bitcast.41, bf16[]{:T(256)} %constant.158.clone.1), dimensions={0}, to_apply=%region_30.31 | reduce | flops 41615360 | bytes 84541440 | tf_op jit(solution)/shard_map/reduce_sum | solution.py:96
  463.1 5.0 fusion.17
  468.1 1.2 constant_dynamic-update-slice_fusion.1
  469.3 127.2 %while.11 = (s32[]{:T(128)}, bf16[2,128,1280]{2,1,0:T(8,128)(2,1)S(1)}, s32[2,16]{1,0:T(2,128)S(1)}, bf16[22,128,2560]{2,1,0:T(8,128)(2,1)}, s32[2]{0:T(128)S(1)...) while((s32[]{:T(128)}, bf16[2,128,1280]{2,1,0:T(8,128)(2,1)S(1)}, ...), condition=%wide.region_36.37_spmd.clone, body=%wide.region_33.36_spmd.clone.sunk | while | flops 1538428160 | bytes 123626600 | solution.py:148
  470.9 11.3 %gather_fusion = bf16[18,128,2560]{2,1,0:T(8,128)(2,1)} fusion(bf16[22,128,2560]{2,1,0:T(8,128)(2,1)} %get-tuple-element.205, s32[1024]{0:T(1024)S(1)} %pad_clamp_fusion.8), kind=kCustom, calls=%fused_computation.clone.clone.1 | custom fusion | bytes 23593032 | tf_op jit(solution)/shard_map/while/body/eval_jaxpr/gather | solution.py:143
  482.2 9.8 %fusion.102 = (bf16[2304,1280]{1,0:T(8,128)(2,1)}, bf16[2304,1280]{1,0:T(8,128)(2,1)}) fusion(bf16[2304,2560]{1,0:T(8,128)(2,1)} %bitcast.167), kind=kLoop, calls=%fused_computation.186.clone.1 | loop fusion | bytes 23592960 | tf_op jit(solution)/shard_map/while/body/eval_jaxpr/slice | solution.py:53
  492.0 8.9 %copy.37 = bf16[2304,1280]{0,1:T(8,128)(2,1)} copy(bf16[2304,1280]{1,0:T(8,128)(2,1)} %get-tuple-element.182) | data formatting | bytes 11796480 | tf_op jit(solution)/shard_map/while
  500.9 8.9 %copy.39 = bf16[2304,1280]{0,1:T(8,128)(2,1)} copy(bf16[2304,1280]{1,0:T(8,128)(2,1)} %get-tuple-element.183) | data formatting | bytes 11796480 | tf_op jit(solution)/shard_map/while
  509.8 11.3 %fusion.103 = (f32[16,128]{1,0:T(8,128)S(1)}, f32[16,128,2304]{2,1,0:T(8,128)}) fusion(pred[2304]{0:T(1024)(128)(4,1)S(1)} %broadcast_bitcast_fusion.2, bf16[128,16,80]{0,2,1:T(8,128)(2,1)S(1)} %bitcast.175, bf16[2304,16,80]{0,2,1:T(8,128)(2,1)} %bitcast.169), kind=kOutput, calls=%fused_computation.187.clone.1 | convolution fusion | flops 773851392 | bytes 25110784 | tf_op jit(solution)/shard_map/while/body/eval_jaxpr/sub | solution.py:60
  521.1 11.5 %fusion.104 = bf16[16,80,128]{2,1,0:T(8,128)(2,1)S(1)} fusion(bf16[2304,16,80]{0,2,1:T(8,128)(2,1)} %bitcast.168, f32[16,128,2304]{2,1,0:T(8,128)} %get-tuple-element.184, f32[16,128]{1,0:T(8,128)S(1)} %get-tuple-element.185), kind=kOutput, calls=%fused_computation.19.clone.1 | convolution fusion | flops 764575744 | bytes 25108480 | tf_op jit(solution)/shard_map/while/body/eval_jaxpr/hqk,khd->qhd/dot_general | solution.py:62
  534.6 11.3 %gather_fusion = bf16[18,128,2560]{2,1,0:T(8,128)(2,1)} fusion(bf16[22,128,2560]{2,1,0:T(8,128)(2,1)} %get-tuple-element.205, s32[1024]{0:T(1024)S(1)} %pad_clamp_fusion.8), kind=kCustom, calls=%fused_computation.clone.clone.1 | custom fusion | bytes 23593032 | tf_op jit(solution)/shard_map/while/body/eval_jaxpr/gather | solution.py:143
  545.8 9.8 %fusion.102 = (bf16[2304,1280]{1,0:T(8,128)(2,1)}, bf16[2304,1280]{1,0:T(8,128)(2,1)}) fusion(bf16[2304,2560]{1,0:T(8,128)(2,1)} %bitcast.167), kind=kLoop, calls=%fused_computation.186.clone.1 | loop fusion | bytes 23592960 | tf_op jit(solution)/shard_map/while/body/eval_jaxpr/slice | solution.py:53
  555.6 8.9 %copy.37 = bf16[2304,1280]{0,1:T(8,128)(2,1)} copy(bf16[2304,1280]{1,0:T(8,128)(2,1)} %get-tuple-element.182) | data formatting | bytes 11796480 | tf_op jit(solution)/shard_map/while
  564.5 8.9 %copy.39 = bf16[2304,1280]{0,1:T(8,128)(2,1)} copy(bf16[2304,1280]{1,0:T(8,128)(2,1)} %get-tuple-element.183) | data formatting | bytes 11796480 | tf_op jit(solution)/shard_map/while
  573.4 11.3 %fusion.103 = (f32[16,128]{1,0:T(8,128)S(1)}, f32[16,128,2304]{2,1,0:T(8,128)}) fusion(pred[2304]{0:T(1024)(128)(4,1)S(1)} %broadcast_bitcast_fusion.2, bf16[128,16,80]{0,2,1:T(8,128)(2,1)S(1)} %bitcast.175, bf16[2304,16,80]{0,2,1:T(8,128)(2,1)} %bitcast.169), kind=kOutput, calls=%fused_computation.187.clone.1 | convolution fusion | flops 773851392 | bytes 25110784 | tf_op jit(solution)/shard_map/while/body/eval_jaxpr/sub | solution.py:60
  584.7 11.6 %fusion.104 = bf16[16,80,128]{2,1,0:T(8,128)(2,1)S(1)} fusion(bf16[2304,16,80]{0,2,1:T(8,128)(2,1)} %bitcast.168, f32[16,128,2304]{2,1,0:T(8,128)} %get-tuple-element.184, f32[16,128]{1,0:T(8,128)S(1)} %get-tuple-element.185), kind=kOutput, calls=%fused_computation.19.clone.1 | convolution fusion | flops 764575744 | bytes 25108480 | tf_op jit(solution)/shard_map/while/body/eval_jaxpr/hqk,khd->qhd/dot_general | solution.py:62
  596.5 3.9 convolution_convert_fusion.1
  (110 shorter events, 12.4 us)
Async XLA Ops:
  6.5 2.9 copy-start
  6.5 99.9 %all-gather.7.cloned.1.call-start = ((), (), s32[]{:S(2)}) async-start(), calls=%async_computation | async-start | bytes 12288000 | tf_op jit(solution)/shard_map/all_gather | solution.py:97
  7.3 3.5 copy-start.2
  7.3 165.4 %all-gather.9.cloned.1.call-start = ((), (), s32[]{:S(2)}) async-start(), calls=%async_computation.1 | async-start | bytes 6553600 | tf_op jit(solution)/shard_map/all_gather | solution.py:108
  10.7 1.3 copy-start.4
  113.1 90.9 %copy-start.3 = (bf16[256,3840]{1,0:T(8,128)(2,1)}, bf16[256,3840]{1,0:T(8,128)(2,1)S(1)}, u32[]{:S(2)}) copy-start(bf16[256,3840]{1,0:T(8,128)(2,1)S(1)} %convolution_convert_fusion) | copy-start | bytes 5898244
  113.1 1.4 copy-start.6
  114.3 7.6 %copy-start.5 = (s32[2,16]{1,0:T(2,128)S(1)}, s32[2,16]{1,0:T(2,128)}, u32[]{:S(2)}) copy-start(s32[2,16]{1,0:T(2,128)} %param.15) | copy-start | bytes 388
  114.4 320.7 %all-gather.13.cloned.1.call-start = ((), (), s32[]{:S(2)}) async-start(), calls=%async_computation.3 | async-start | bytes 84541440 | tf_op jit(solution)/shard_map/all_gather | solution.py:95
  121.2 475.3 %all-gather.11.cloned.1.call-start = ((), (), s32[]{:S(2)}) async-start(), calls=%async_computation.2 | async-start | bytes 4096000 | tf_op jit(solution)/shard_map/all_gather | solution.py:153
  177.1 54.9 %collective-permute-start = (bf16[3,128,2560]{2,1,0:T(8,128)(2,1)}, bf16[3,128,2560]{2,1,0:T(8,128)(2,1)}, u32[]{:S(2)}, u32[]{:S(2)}) collective-permute-start(bf16[3,128,2560]{2,1,0:T(8,128)(2,1)} %gather_fusion.4), channel_id=1, source_target_pairs={{0,8},{4,12},{8,16},{12,20},{16,24},{20,28},{24,32},{28,36},{32,40... | collective-permute-start | bytes 5898248 | tf_op jit(solution)/shard_map/ppermute | solution.py:18
  185.0 66.7 %collective-permute-start.1 = (bf16[3,128,2560]{2,1,0:T(8,128)(2,1)}, bf16[3,128,2560]{2,1,0:T(8,128)(2,1)}, u32[]{:S(2)}, u32[]{:S(2)}) collective-permute-start(bf16[3,128,2560]{2,1,0:T(8,128)(2,1)} %gather_fusion.5), channel_id=1, source_target_pairs={{0,4},{4,8},{8,12},{12,16},{16,20},{20,24},{24,28},{28,32},{32,36}... | collective-permute-start | bytes 5898248 | tf_op jit(solution)/shard_map/ppermute | solution.py:18
  191.7 63.1 %collective-permute-start.2 = (bf16[3,128,2560]{2,1,0:T(8,128)(2,1)}, bf16[3,128,2560]{2,1,0:T(8,128)(2,1)}, u32[]{:S(2)}, u32[]{:S(2)}) collective-permute-start(bf16[3,128,2560]{2,1,0:T(8,128)(2,1)} %gather_fusion.6), channel_id=1, source_target_pairs={{4,0},{8,4},{12,8},{16,12},{20,16},{24,20},{28,24},{32,28},{36,32}... | collective-permute-start | bytes 5898248 | tf_op jit(solution)/shard_map/ppermute | solution.py:18
  200.1 64.9 %collective-permute-start.3 = (bf16[3,128,2560]{2,1,0:T(8,128)(2,1)}, bf16[3,128,2560]{2,1,0:T(8,128)(2,1)}, u32[]{:S(2)}, u32[]{:S(2)}) collective-permute-start(bf16[3,128,2560]{2,1,0:T(8,128)(2,1)} %gather_fusion.7), channel_id=1, source_target_pairs={{8,0},{12,4},{16,8},{20,12},{24,16},{28,20},{32,24},{36,28},{40,32... | collective-permute-start | bytes 5898248 | tf_op jit(solution)/shard_map/ppermute | solution.py:18
  463.0 6.2 %slice-start = ((bf16[256,3840]{1,0:T(8,128)(2,1)}), bf16[256,1280]{1,0:T(8,128)(2,1)S(1)}, s32[]{:S(2)}) async-start(bf16[256,3840]{1,0:T(8,128)(2,1)} %copy-done.3), calls=%async_computation.4 | async-start | bytes 1310720 | tf_op jit(solution)/shard_map/slice | solution.py:100
  463.0 6.2 %copy-start.7 = (bf16[2,128,1280]{2,1,0:T(8,128)(2,1)S(1)}, bf16[2,128,1280]{2,1,0:T(8,128)(2,1)}, u32[]{:S(2)}) copy-start(bf16[2,128,1280]{2,1,0:T(8,128)(2,1)} %custom-call.17) | copy-start | bytes 1966084
  463.0 6.2 %copy-start.8 = (s32[2]{0:T(128)S(1)}, s32[2]{0:T(128)}, u32[]{:S(2)}) copy-start(s32[2]{0:T(128)} %param.16) | copy-start | bytes 28
  596.5 3.9 copy-start.1
Sparse Core Ops, SparseCore 0:
  9.0 97.3 all-gather.6
  114.5 58.1 all-gather.8
  175.6 259.3 all-gather.12
  436.5 39.7 all-gather.10
